TPU v7x, 256 devices: a whole 4x4x8 slice. The times are simulated.
256 devices in a mesh: gz: 32 (over z, y_hi, core), ch: 8 (over y_lo, x).
Axes of the slice: x: 4, y: 4 (y_hi: 2, y_lo: 2; y = y_hi * 2 + y_lo), z: 8, core: 2. Of those that a mesh axis runs over, the one named last changes fastest.
Arguments:
- volume: bfloat16 [64, 1024, 512], P('ch', 'gz'), may hold values from -6 to 6
- plane_a: bfloat16 [2, 64, 64, 3, 3], P(None, 'ch'), may hold values from -0.375 to 0.375
- plane_b: bfloat16 [2, 64, 64, 3, 3], P(None, 'ch'), may hold values from -0.375 to 0.375
- depth: bfloat16 [2, 64, 64, 3], P(None, 'ch'), may hold values from -0.625 to 0.625
Outputs:
- features: bfloat16 [64, 1024, 512], P('ch', 'gz')
All inputs are finite; a program needn't handle non-finite values.
Results may differ from a plain program's by a relative error of at most 0.015.
Values may be sent and summed in bfloat16 or wider, within the bound.
No kernel may reach another device: no remote copies, remote signals or barrier semaphores. Data moves between devices by JAX's collectives and lax.ppermute only.
A program may use at most 64 MiB of HBM per device.

v0:
```python
import jax
import jax.numpy as jnp
from jax import lax
from jax.sharding import PartitionSpec as P

X = 64
Y = 8


def from_behind(block, axis, distance):
    devices = range(lax.axis_size(axis))
    route = [(i - distance, i) for i in devices if i - distance in devices]
    return lax.ppermute(block, axis, route)


def gather_weights(plane_a, plane_b, depth):
    return (
        lax.all_gather(plane_a, "ch", axis=1, tiled=True),
        lax.all_gather(plane_b, "ch", axis=1, tiled=True),
        lax.all_gather(depth, "ch", axis=1, tiled=True),
    )


def plane_conv(h, weight):
    out = lax.conv_general_dilated(
        h,
        weight,
        (1, 1),
        ((1, 1), (1, 1)),
        dimension_numbers=("CNHW", "OIHW", "CNHW"),
        preferred_element_type=jnp.float32,
    )
    return jnp.maximum(out, 0.0).astype(jnp.bfloat16)


def depth_conv(second, weight):
    lower = from_behind(second, "gz", 2)
    upper = from_behind(second, "gz", -2)
    total = jnp.einsum("oi,isxy->osxy", weight[:, :, 1], second, preferred_element_type=jnp.float32)
    total = total + jnp.einsum(
        "oi,isxy->osxy", weight[:, :, 0], lower, preferred_element_type=jnp.float32
    )
    total = total + jnp.einsum(
        "oi,isxy->osxy", weight[:, :, 2], upper, preferred_element_type=jnp.float32
    )
    return jnp.maximum(total, 0.0).astype(jnp.bfloat16)


def local(volume, plane_a, plane_b, depth):
    full_a, full_b, full_d = gather_weights(plane_a, plane_b, depth)
    part, slab, flat = volume.shape
    h = lax.all_to_all(volume, "ch", split_axis=1, concat_axis=0, tiled=True)
    chans, slices = h.shape[:2]
    h = h.reshape(chans, slices, X, Y)
    for layer_index in range(plane_a.shape[0]):
        first = plane_conv(h, full_a[layer_index])
        second = plane_conv(first, full_b[layer_index])
        h = depth_conv(second, full_d[layer_index])
    h = h.reshape(chans, slices, flat)
    return lax.all_to_all(h, "ch", split_axis=0, concat_axis=1, tiled=True)


def solution(mesh):
    return jax.shard_map(
        local,
        mesh=mesh,
        in_specs=(
            P("ch", "gz", None),
            P(None, "ch", None, None, None),
            P(None, "ch", None, None, None),
            P(None, "ch", None, None),
        ),
        out_specs=P("ch", "gz", None),
        check_vma=False,
    )
```

profile of v0, /device:TPU:96, one launch (start us, length us, event | category | flops | bytes accessed | tf_op | source)
XLA Modules:
  0.0 164.3 jit_solution(17486440112829499366)
XLA Ops:
  0.0 1.8 %copy.37 = bf16[8,32,512]{2,0,1:T(8,128)(2,1)} copy(bf16[8,32,512]{2,1,0:T(8,128)(2,1)} %param.4) | data formatting | bytes 524288 | tf_op args[0]
  1.8 5.3 %all-to-all-start = ((bf16[8,32,512]{2,0,1:T(8,128)(2,1)}), bf16[8,32,512]{2,0,1:T(8,128)(2,1)S(1)}, u32[]{:S(2)}, u32[]{:S(2)}) async-start(bf16[8,32,512]{2,0,1:T(8,128)(2,1)} %copy.37), calls=%async_computation | async-start | bytes 524288 | tf_op jit(solution)/shard_map/all_to_all | solution.py:52
  7.1 25.9 %all_gather.10 = bf16[2,64,64,3,3]{2,1,4,3,0:T(8,128)(2,1)S(1)} all-gather(bf16[2,8,64,3,3]{2,1,4,3,0:T(8,128)(2,1)} %param.6), channel_id=1, replica_groups=mesh['gz'=32,'ch'=8] {'ch'}, dimensions={1}, use_global_device_ids=true | all-gather | bytes 165888 | tf_op jit(solution)/shard_map/all_gather | solution.py:19
  33.0 24.8 %all_gather.9 = bf16[2,64,64,3,3]{2,1,4,3,0:T(8,128)(2,1)S(1)} all-gather(bf16[2,8,64,3,3]{2,1,4,3,0:T(8,128)(2,1)} %param.5), channel_id=1, replica_groups=mesh['gz'=32,'ch'=8] {'ch'}, dimensions={1}, use_global_device_ids=true | all-gather | bytes 165888 | tf_op jit(solution)/shard_map/all_gather | solution.py:18
  57.9 23.9 %all_gather.11 = bf16[2,64,64,3]{2,1,3,0:T(8,128)(2,1)S(1)} all-gather(bf16[2,8,64,3]{2,1,3,0:T(8,128)(2,1)} %param.7), channel_id=1, replica_groups=mesh['gz'=32,'ch'=8] {'ch'}, dimensions={1}, use_global_device_ids=true | all-gather | bytes 55296 | tf_op jit(solution)/shard_map/all_gather | solution.py:20
  81.8 5.9 %reshape.7 = bf16[64,4,64,8]{3,2,0,1:T(8,128)(2,1)} reshape(bf16[8,8,4,512]{3,1,0,2:T(8,128)(2,1)S(1)} %bitcast.81) | data formatting | bytes 524288 | tf_op jit(solution)/shard_map/reshape | solution.py:54
  87.7 5.7 %copy.39 = bf16[64,4,64,8]{0,1,3,2:T(4,128)(2,1)S(1)} copy(bf16[64,4,64,8]{3,2,0,1:T(8,128)(2,1)} %reshape.7) | data formatting | bytes 524288 | tf_op jit(solution)/shard_map/reshape | solution.py:54
  93.4 5.5 %fusion.5 = bf16[64,4,64,8]{0,1,3,2:T(4,128)(2,1)S(1)} fusion(bf16[64,4,64,8]{0,1,3,2:T(4,128)(2,1)S(1)} %copy.39, bf16[2,64,64,3,3]{2,1,4,3,0:T(8,128)(2,1)S(1)} %all_gather.10, bf16[2,64,64,3,3]{2,1,4,3,0:T(8,128)(2,1)S(1)} %all_gather.9), kind=kOutput, calls=%fused_computation.13 | convolution fusion | flops 274464768 | bytes 1081344 | tf_op jit(solution)/shard_map/conv_general_dilated | solution.py:25
  98.8 4.8 %collective-permute-start = (bf16[64,4,64,8]{0,1,3,2:T(4,128)(2,1)S(1)}, bf16[64,4,64,8]{0,1,3,2:T(4,128)(2,1)S(1)}, u32[]{:S(2)}, u32[]{:S(2)}) collective-permute-start(bf16[64,4,64,8]{0,1,3,2:T(4,128)(2,1)S(1)} %fusion.5), channel_id=1, source_target_pairs={{0,16},{8,24},{16,32},{24,40},{32,48},{40,56},{48,64},{56,72},{64,... | collective-permute-start | bytes 786440 | tf_op jit(solution)/shard_map/ppermute | solution.py:13
  103.7 3.6 %collective-permute-start.1 = (bf16[64,4,64,8]{0,1,3,2:T(4,128)(2,1)S(1)}, bf16[64,4,64,8]{0,1,3,2:T(4,128)(2,1)S(1)}, u32[]{:S(2)}, u32[]{:S(2)}) collective-permute-start(bf16[64,4,64,8]{0,1,3,2:T(4,128)(2,1)S(1)} %fusion.5), channel_id=1, source_target_pairs={{16,0},{24,8},{32,16},{40,24},{48,32},{56,40},{64,48},{72,56},{80,... | collective-permute-start | bytes 786440 | tf_op jit(solution)/shard_map/ppermute | solution.py:13
  107.3 0.4 fusion.16
  107.7 4.7 %collective-permute-done = bf16[64,4,64,8]{0,1,3,2:T(4,128)(2,1)S(1)} collective-permute-done((bf16[64,4,64,8]{0,1,3,2:T(4,128)(2,1)S(1)}, bf16[64,4,64,8]{0,1,3,2:T(4,128)(2,1)S(1)}, u32[]{:S(2)}, u32[]{:S(2)}) %collective-permute-start) | collective-permute-done | bytes 262176 | tf_op jit(solution)/shard_map/ppermute | solution.py:13
  112.4 0.4 convolution_add_fusion.3
  112.8 12.6 %collective-permute-done.1 = bf16[64,4,64,8]{0,1,3,2:T(4,128)(2,1)S(1)} collective-permute-done((bf16[64,4,64,8]{0,1,3,2:T(4,128)(2,1)S(1)}, bf16[64,4,64,8]{0,1,3,2:T(4,128)(2,1)S(1)}, u32[]{:S(2)}, u32[]{:S(2)}) %collective-permute-start.1) | collective-permute-done | bytes 262176 | tf_op jit(solution)/shard_map/ppermute | solution.py:13
  125.5 0.4 fusion.2
  125.9 5.5 %fusion.7 = bf16[64,4,64,8]{0,1,3,2:T(4,128)(2,1)S(1)} fusion(bf16[4,64,8,64]{3,1,2,0:T(8,128)(2,1)S(1)} %fusion.2, bf16[2,64,64,3,3]{2,1,4,3,0:T(8,128)(2,1)S(1)} %all_gather.10, bf16[2,64,64,3,3]{2,1,4,3,0:T(8,128)(2,1)S(1)} %all_gather.9), kind=kOutput, calls=%fused_computation.15 | convolution fusion | flops 274464768 | bytes 1081344 | tf_op jit(solution)/shard_map/conv_general_dilated | solution.py:25
  131.4 1.9 %collective-permute-start.2 = (bf16[64,4,64,8]{0,1,3,2:T(4,128)(2,1)S(1)}, bf16[64,4,64,8]{0,1,3,2:T(4,128)(2,1)S(1)}, u32[]{:S(2)}, u32[]{:S(2)}) collective-permute-start(bf16[64,4,64,8]{0,1,3,2:T(4,128)(2,1)S(1)} %fusion.7), channel_id=1, source_target_pairs={{0,16},{8,24},{16,32},{24,40},{32,48},{40,56},{48,64},{56,72},{64,... | collective-permute-start | bytes 786440 | tf_op jit(solution)/shard_map/ppermute | solution.py:13
  133.4 6.3 %collective-permute-start.3 = (bf16[64,4,64,8]{0,1,3,2:T(4,128)(2,1)S(1)}, bf16[64,4,64,8]{0,1,3,2:T(4,128)(2,1)S(1)}, u32[]{:S(2)}, u32[]{:S(2)}) collective-permute-start(bf16[64,4,64,8]{0,1,3,2:T(4,128)(2,1)S(1)} %fusion.7), channel_id=1, source_target_pairs={{16,0},{24,8},{32,16},{40,24},{48,32},{56,40},{64,48},{72,56},{80,... | collective-permute-start | bytes 786440 | tf_op jit(solution)/shard_map/ppermute | solution.py:13
  140.1 6.0 %collective-permute-done.2 = bf16[64,4,64,8]{0,1,3,2:T(4,128)(2,1)S(1)} collective-permute-done((bf16[64,4,64,8]{0,1,3,2:T(4,128)(2,1)S(1)}, bf16[64,4,64,8]{0,1,3,2:T(4,128)(2,1)S(1)}, u32[]{:S(2)}, u32[]{:S(2)}) %collective-permute-start.2) | collective-permute-done | bytes 262176 | tf_op jit(solution)/shard_map/ppermute | solution.py:13
  146.1 0.4 convolution_add_fusion.1
  146.5 5.1 %collective-permute-done.3 = bf16[64,4,64,8]{0,1,3,2:T(4,128)(2,1)S(1)} collective-permute-done((bf16[64,4,64,8]{0,1,3,2:T(4,128)(2,1)S(1)}, bf16[64,4,64,8]{0,1,3,2:T(4,128)(2,1)S(1)}, u32[]{:S(2)}, u32[]{:S(2)}) %collective-permute-start.3) | collective-permute-done | bytes 262176 | tf_op jit(solution)/shard_map/ppermute | solution.py:13
  151.6 0.4 fusion.8
  152.6 10.8 %all_to_all.33 = bf16[64,4,512]{2,1,0:T(4,128)(2,1)S(1)} all-to-all(bf16[64,4,512]{2,1,0:T(4,128)(2,1)S(1)} %copy.48), channel_id=1, replica_groups=mesh['gz'=32,'ch'=8] {'ch'}, dimensions={0} | all-to-all | bytes 524288 | tf_op jit(solution)/shard_map/all_to_all | solution.py:60
  163.5 0.8 copy.51
  (8 shorter events, 1.1 us)
Async XLA Ops:
  1.8 80.0 %all-to-all-start = ((bf16[8,32,512]{2,0,1:T(8,128)(2,1)}), bf16[8,32,512]{2,0,1:T(8,128)(2,1)S(1)}, u32[]{:S(2)}, u32[]{:S(2)}) async-start(bf16[8,32,512]{2,0,1:T(8,128)(2,1)} %copy.37), calls=%async_computation | async-start | bytes 524288 | tf_op jit(solution)/shard_map/all_to_all | solution.py:52
  98.8 13.6 %collective-permute-start = (bf16[64,4,64,8]{0,1,3,2:T(4,128)(2,1)S(1)}, bf16[64,4,64,8]{0,1,3,2:T(4,128)(2,1)S(1)}, u32[]{:S(2)}, u32[]{:S(2)}) collective-permute-start(bf16[64,4,64,8]{0,1,3,2:T(4,128)(2,1)S(1)} %fusion.5), channel_id=1, source_target_pairs={{0,16},{8,24},{16,32},{24,40},{32,48},{40,56},{48,64},{56,72},{64,... | collective-permute-start | bytes 786440 | tf_op jit(solution)/shard_map/ppermute | solution.py:13
  103.7 21.8 %collective-permute-start.1 = (bf16[64,4,64,8]{0,1,3,2:T(4,128)(2,1)S(1)}, bf16[64,4,64,8]{0,1,3,2:T(4,128)(2,1)S(1)}, u32[]{:S(2)}, u32[]{:S(2)}) collective-permute-start(bf16[64,4,64,8]{0,1,3,2:T(4,128)(2,1)S(1)} %fusion.5), channel_id=1, source_target_pairs={{16,0},{24,8},{32,16},{40,24},{48,32},{56,40},{64,48},{72,56},{80,... | collective-permute-start | bytes 786440 | tf_op jit(solution)/shard_map/ppermute | solution.py:13
  131.4 14.6 %collective-permute-start.2 = (bf16[64,4,64,8]{0,1,3,2:T(4,128)(2,1)S(1)}, bf16[64,4,64,8]{0,1,3,2:T(4,128)(2,1)S(1)}, u32[]{:S(2)}, u32[]{:S(2)}) collective-permute-start(bf16[64,4,64,8]{0,1,3,2:T(4,128)(2,1)S(1)} %fusion.7), channel_id=1, source_target_pairs={{0,16},{8,24},{16,32},{24,40},{32,48},{40,56},{48,64},{56,72},{64,... | collective-permute-start | bytes 786440 | tf_op jit(solution)/shard_map/ppermute | solution.py:13
  133.4 18.2 %collective-permute-start.3 = (bf16[64,4,64,8]{0,1,3,2:T(4,128)(2,1)S(1)}, bf16[64,4,64,8]{0,1,3,2:T(4,128)(2,1)S(1)}, u32[]{:S(2)}, u32[]{:S(2)}) collective-permute-start(bf16[64,4,64,8]{0,1,3,2:T(4,128)(2,1)S(1)} %fusion.7), channel_id=1, source_target_pairs={{16,0},{24,8},{32,16},{40,24},{48,32},{56,40},{64,48},{72,56},{80,... | collective-permute-start | bytes 786440 | tf_op jit(solution)/shard_map/ppermute | solution.py:13
where the time goes:
time: 165 us; the launch traced here: 164 us
  blocking collectives  85.4 us (52%)
  waiting for transfers between devices  28.4 us (17%)
  starting transfers between devices  22 us (13%)
  local copies, waits for them, and re-layouts  14.9 us (9%)
  matrix products  13.4 us (8%)
    ppermute x4, waiting for transfers between devices, from_behind(): return lax.ppermute(block, axis, route)  28.4 us
    all_gather x1, blocking collectives, gather_weights(): lax.all_gather(plane_b, 'ch', axis=1, tiled=True)  25.9 us
    all_gather x1, blocking collectives, gather_weights(): lax.all_gather(plane_a, 'ch', axis=1, tiled=True)  24.8 us
    all_gather x1, blocking collectives, gather_weights(): lax.all_gather(depth, 'ch', axis=1, tiled=True)  23.9 us
    ppermute x4, starting transfers between devices, from_behind(): return lax.ppermute(block, axis, route)  16.7 us
    reshape x2, local copies, waits for them, and re-layouts, local(): h = h.reshape(chans, slices, X, Y)  11.6 us
    conv_general_dilated x2, matrix products, plane_conv(): lax.conv_general_dilated(h, weight, (1, 1), ((1, 1), (1, 1)), dimension_n...  11 us
    all_to_all x1, blocking collectives, local(): return lax.all_to_all(h, 'ch', split_axis=0, concat_axis=1, tiled=True)  10.8 us
  transfers between devices with their start and end apart: 5, of which 4 were waited for; matrix products, arithmetic and copies ran while one was open for 1% of the time, Pallas kernels for 0%

commit v1 on v0

--- a/solution.py
+++ b/solution.py
@@ -15,7 +15,9 @@
 
 def gather_weights(plane_a, plane_b, depth):
     return (
-        lax.all_gather(plane_a, "ch", axis=1, tiled=True),
+        jnp.concatenate(
+            lax.all_to_all(jnp.stack([plane_a] * lax.axis_size("ch")), "ch", 0, 0), axis=1
+        ),
         lax.all_gather(plane_b, "ch", axis=1, tiled=True),
         lax.all_gather(depth, "ch", axis=1, tiled=True),
     )

time: 165 us -> 147 us (0.89)
  the two profiles are of different devices: /device:TPU:96 before, /device:TPU:128 now
where the time goes in v1:
time: 147 us
  blocking collectives  59.9 us (41%)
  waiting for transfers between devices  28.2 us (19%)
  starting transfers between devices  27.8 us (19%)
  local copies, waits for them, and re-layouts  17 us (12%)
  matrix products  13.6 us (9%)
    all_gather x1, blocking collectives, gather_weights(): lax.all_gather(plane_b, 'ch', axis=1, tiled=True)  25.2 us
    all_gather x1, blocking collectives, gather_weights(): lax.all_gather(depth, 'ch', axis=1, tiled=True)  24.9 us
    ppermute x4, waiting for transfers between devices, from_behind(): return lax.ppermute(block, axis, route)  21.3 us
    ppermute x4, starting transfers between devices, from_behind(): return lax.ppermute(block, axis, route)  19.1 us
    reshape x2, local copies, waits for them, and re-layouts, local(): h = h.reshape(chans, slices, X, Y)  11.7 us
    conv_general_dilated x2, matrix products, plane_conv(): lax.conv_general_dilated(h, weight, (1, 1), ((1, 1), (1, 1)), dimension_n...  11.1 us
    all_to_all x1, blocking collectives, local(): return lax.all_to_all(h, 'ch', split_axis=0, concat_axis=1, tiled=True)  9.81 us
    all_to_all x1, waiting for transfers between devices, local(): h = lax.all_to_all(volume, 'ch', split_axis=1, concat_axis=0, tiled=True)  6.91 us
  transfers between devices with their start and end apart: 6, of which 5 were waited for; matrix products, arithmetic and copies ran while one was open for 3% of the time, Pallas kernels for 0%

profile of v1, /device:TPU:128, one launch (start us, length us, event | category | flops | bytes accessed | tf_op | source)
XLA Modules:
  0.0 146.6 jit_solution(15589182646225962946)
XLA Ops:
  0.0 0.8 copy-done
  0.8 0.9 reshape.26
  1.7 5.3 %all-to-all-start.1 = ((bf16[8,2,4608]{2,1,0:T(2,128)(2,1)}), bf16[8,2,4608]{2,1,0:T(2,128)(2,1)S(1)}, u32[]{:S(2)}, u32[]{:S(2)}) async-start(bf16[8,2,4608]{2,1,0:T(2,128)(2,1)} %reshape.26), calls=%async_computation.1 | async-start | bytes 294912 | tf_op jit(solution)/shard_map/all_to_all | solution.py:19
  7.0 24.9 %all_gather.7 = bf16[2,64,64,3]{2,1,3,0:T(8,128)(2,1)S(1)} all-gather(bf16[2,8,64,3]{2,1,3,0:T(8,128)(2,1)} %param.7), channel_id=1, replica_groups=mesh['gz'=32,'ch'=8] {'ch'}, dimensions={1}, use_global_device_ids=true | all-gather | bytes 55296 | tf_op jit(solution)/shard_map/all_gather | solution.py:22
  31.9 1.8 %copy.37 = bf16[8,32,512]{2,0,1:T(8,128)(2,1)} copy(bf16[8,32,512]{2,1,0:T(8,128)(2,1)} %param.4) | data formatting | bytes 524288 | tf_op args[0]
  33.7 25.2 %all_gather.6 = bf16[2,64,64,3,3]{2,1,4,3,0:T(8,128)(2,1)S(1)} all-gather(bf16[2,8,64,3,3]{2,1,4,3,0:T(8,128)(2,1)} %param.6), channel_id=1, replica_groups=mesh['gz'=32,'ch'=8] {'ch'}, dimensions={1}, use_global_device_ids=true | all-gather | bytes 165888 | tf_op jit(solution)/shard_map/all_gather | solution.py:21
  58.9 3.4 %all-to-all-start = ((bf16[8,32,512]{2,0,1:T(8,128)(2,1)}), bf16[8,32,512]{2,0,1:T(8,128)(2,1)S(1)}, u32[]{:S(2)}, u32[]{:S(2)}) async-start(bf16[8,32,512]{2,0,1:T(8,128)(2,1)} %copy.37), calls=%async_computation | async-start | bytes 524288 | tf_op jit(solution)/shard_map/all_to_all | solution.py:54
  62.7 6.9 %all-to-all-done = bf16[8,32,512]{2,0,1:T(8,128)(2,1)S(1)} async-done(((bf16[8,32,512]{2,0,1:T(8,128)(2,1)}), bf16[8,32,512]{2,0,1:T(8,128)(2,1)S(1)}, u32[]{:S(2)}, u32[]{:S(2)}) %all-to-all-start) | async-done | bytes 262176 | tf_op jit(solution)/shard_map/all_to_all | solution.py:54
  69.6 5.9 %reshape.17 = bf16[64,4,64,8]{3,2,0,1:T(8,128)(2,1)} reshape(bf16[8,8,4,512]{3,1,0,2:T(8,128)(2,1)S(1)} %bitcast.87) | data formatting | bytes 524288 | tf_op jit(solution)/shard_map/reshape | solution.py:56
  75.5 5.8 %copy.40 = bf16[64,4,64,8]{0,1,3,2:T(4,128)(2,1)S(1)} copy(bf16[64,4,64,8]{3,2,0,1:T(8,128)(2,1)} %reshape.17) | data formatting | bytes 524288 | tf_op jit(solution)/shard_map/reshape | solution.py:56
  81.3 5.5 %fusion.5 = bf16[64,4,64,8]{0,1,3,2:T(4,128)(2,1)S(1)} fusion(bf16[64,4,64,8]{0,1,3,2:T(4,128)(2,1)S(1)} %copy.40, bf16[2,64,64,3,3]{2,1,4,3,0:T(8,128)(2,1)S(1)} %all_gather.6, bf16[1,8,8,64,3,3]{3,2,5,4,0,1:T(8,128)(2,1)S(1)} %get-tuple-element.6), kind=kOutput, calls=%fused_computation.13 | convolution fusion | flops 274464768 | bytes 1081344 | tf_op jit(solution)/shard_map/conv_general_dilated | solution.py:27
  86.8 4.8 %collective-permute-start = (bf16[64,4,64,8]{0,1,3,2:T(4,128)(2,1)S(1)}, bf16[64,4,64,8]{0,1,3,2:T(4,128)(2,1)S(1)}, u32[]{:S(2)}, u32[]{:S(2)}) collective-permute-start(bf16[64,4,64,8]{0,1,3,2:T(4,128)(2,1)S(1)} %fusion.5), channel_id=1, source_target_pairs={{0,16},{8,24},{16,32},{24,40},{32,48},{40,56},{48,64},{56,72},{64,... | collective-permute-start | bytes 786440 | tf_op jit(solution)/shard_map/ppermute | solution.py:13
  91.7 4.8 %collective-permute-start.1 = (bf16[64,4,64,8]{0,1,3,2:T(4,128)(2,1)S(1)}, bf16[64,4,64,8]{0,1,3,2:T(4,128)(2,1)S(1)}, u32[]{:S(2)}, u32[]{:S(2)}) collective-permute-start(bf16[64,4,64,8]{0,1,3,2:T(4,128)(2,1)S(1)} %fusion.5), channel_id=1, source_target_pairs={{16,0},{24,8},{32,16},{40,24},{48,32},{56,40},{64,48},{72,56},{80,... | collective-permute-start | bytes 786440 | tf_op jit(solution)/shard_map/ppermute | solution.py:13
  96.9 7.1 %collective-permute-done = bf16[64,4,64,8]{0,1,3,2:T(4,128)(2,1)S(1)} collective-permute-done((bf16[64,4,64,8]{0,1,3,2:T(4,128)(2,1)S(1)}, bf16[64,4,64,8]{0,1,3,2:T(4,128)(2,1)S(1)}, u32[]{:S(2)}, u32[]{:S(2)}) %collective-permute-start) | collective-permute-done | bytes 262176 | tf_op jit(solution)/shard_map/ppermute | solution.py:13
  104.4 2.8 %collective-permute-done.1 = bf16[64,4,64,8]{0,1,3,2:T(4,128)(2,1)S(1)} collective-permute-done((bf16[64,4,64,8]{0,1,3,2:T(4,128)(2,1)S(1)}, bf16[64,4,64,8]{0,1,3,2:T(4,128)(2,1)S(1)}, u32[]{:S(2)}, u32[]{:S(2)}) %collective-permute-start.1) | collective-permute-done | bytes 262176 | tf_op jit(solution)/shard_map/ppermute | solution.py:13
  107.1 0.4 fusion.2
  107.6 5.6 %fusion.7 = bf16[64,4,64,8]{0,1,3,2:T(4,128)(2,1)S(1)} fusion(bf16[4,64,8,64]{3,1,2,0:T(8,128)(2,1)S(1)} %fusion.2, bf16[2,64,64,3,3]{2,1,4,3,0:T(8,128)(2,1)S(1)} %all_gather.6, bf16[1,8,8,64,3,3]{3,2,5,4,0,1:T(8,128)(2,1)S(1)} %get-tuple-element.5), kind=kOutput, calls=%fused_computation.15 | convolution fusion | flops 274464768 | bytes 1081344 | tf_op jit(solution)/shard_map/conv_general_dilated | solution.py:27
  113.2 3.1 %collective-permute-start.2 = (bf16[64,4,64,8]{0,1,3,2:T(4,128)(2,1)S(1)}, bf16[64,4,64,8]{0,1,3,2:T(4,128)(2,1)S(1)}, u32[]{:S(2)}, u32[]{:S(2)}) collective-permute-start(bf16[64,4,64,8]{0,1,3,2:T(4,128)(2,1)S(1)} %fusion.7), channel_id=1, source_target_pairs={{0,16},{8,24},{16,32},{24,40},{32,48},{40,56},{48,64},{56,72},{64,... | collective-permute-start | bytes 786440 | tf_op jit(solution)/shard_map/ppermute | solution.py:13
  116.3 6.3 %collective-permute-start.3 = (bf16[64,4,64,8]{0,1,3,2:T(4,128)(2,1)S(1)}, bf16[64,4,64,8]{0,1,3,2:T(4,128)(2,1)S(1)}, u32[]{:S(2)}, u32[]{:S(2)}) collective-permute-start(bf16[64,4,64,8]{0,1,3,2:T(4,128)(2,1)S(1)} %fusion.7), channel_id=1, source_target_pairs={{16,0},{24,8},{32,16},{40,24},{48,32},{56,40},{64,48},{72,56},{80,... | collective-permute-start | bytes 786440 | tf_op jit(solution)/shard_map/ppermute | solution.py:13
  123.1 7.0 %collective-permute-done.2 = bf16[64,4,64,8]{0,1,3,2:T(4,128)(2,1)S(1)} collective-permute-done((bf16[64,4,64,8]{0,1,3,2:T(4,128)(2,1)S(1)}, bf16[64,4,64,8]{0,1,3,2:T(4,128)(2,1)S(1)}, u32[]{:S(2)}, u32[]{:S(2)}) %collective-permute-start.2) | collective-permute-done | bytes 262176 | tf_op jit(solution)/shard_map/ppermute | solution.py:13
  130.4 4.5 %collective-permute-done.3 = bf16[64,4,64,8]{0,1,3,2:T(4,128)(2,1)S(1)} collective-permute-done((bf16[64,4,64,8]{0,1,3,2:T(4,128)(2,1)S(1)}, bf16[64,4,64,8]{0,1,3,2:T(4,128)(2,1)S(1)}, u32[]{:S(2)}, u32[]{:S(2)}) %collective-permute-start.3) | collective-permute-done | bytes 262176 | tf_op jit(solution)/shard_map/ppermute | solution.py:13
  134.9 0.4 fusion.8
  136.0 9.8 %all_to_all.38 = bf16[64,4,512]{2,1,0:T(4,128)(2,1)S(1)} all-to-all(bf16[64,4,512]{2,1,0:T(4,128)(2,1)S(1)} %copy.50), channel_id=1, replica_groups=mesh['gz'=32,'ch'=8] {'ch'}, dimensions={0} | all-to-all | bytes 524288 | tf_op jit(solution)/shard_map/all_to_all | solution.py:62
  145.9 0.8 copy.53
  (16 shorter events, 2.7 us)
Async XLA Ops:
  0.0 0.8 copy-start
  1.7 57.3 %all-to-all-start.1 = ((bf16[8,2,4608]{2,1,0:T(2,128)(2,1)}), bf16[8,2,4608]{2,1,0:T(2,128)(2,1)S(1)}, u32[]{:S(2)}, u32[]{:S(2)}) async-start(bf16[8,2,4608]{2,1,0:T(2,128)(2,1)} %reshape.26), calls=%async_computation.1 | async-start | bytes 294912 | tf_op jit(solution)/shard_map/all_to_all | solution.py:19
  58.9 10.6 %all-to-all-start = ((bf16[8,32,512]{2,0,1:T(8,128)(2,1)}), bf16[8,32,512]{2,0,1:T(8,128)(2,1)S(1)}, u32[]{:S(2)}, u32[]{:S(2)}) async-start(bf16[8,32,512]{2,0,1:T(8,128)(2,1)} %copy.37), calls=%async_computation | async-start | bytes 524288 | tf_op jit(solution)/shard_map/all_to_all | solution.py:54
  86.8 17.1 %collective-permute-start = (bf16[64,4,64,8]{0,1,3,2:T(4,128)(2,1)S(1)}, bf16[64,4,64,8]{0,1,3,2:T(4,128)(2,1)S(1)}, u32[]{:S(2)}, u32[]{:S(2)}) collective-permute-start(bf16[64,4,64,8]{0,1,3,2:T(4,128)(2,1)S(1)} %fusion.5), channel_id=1, source_target_pairs={{0,16},{8,24},{16,32},{24,40},{32,48},{40,56},{48,64},{56,72},{64,... | collective-permute-start | bytes 786440 | tf_op jit(solution)/shard_map/ppermute | solution.py:13
  91.7 15.5 %collective-permute-start.1 = (bf16[64,4,64,8]{0,1,3,2:T(4,128)(2,1)S(1)}, bf16[64,4,64,8]{0,1,3,2:T(4,128)(2,1)S(1)}, u32[]{:S(2)}, u32[]{:S(2)}) collective-permute-start(bf16[64,4,64,8]{0,1,3,2:T(4,128)(2,1)S(1)} %fusion.5), channel_id=1, source_target_pairs={{16,0},{24,8},{32,16},{40,24},{48,32},{56,40},{64,48},{72,56},{80,... | collective-permute-start | bytes 786440 | tf_op jit(solution)/shard_map/ppermute | solution.py:13
  113.2 16.8 %collective-permute-start.2 = (bf16[64,4,64,8]{0,1,3,2:T(4,128)(2,1)S(1)}, bf16[64,4,64,8]{0,1,3,2:T(4,128)(2,1)S(1)}, u32[]{:S(2)}, u32[]{:S(2)}) collective-permute-start(bf16[64,4,64,8]{0,1,3,2:T(4,128)(2,1)S(1)} %fusion.7), channel_id=1, source_target_pairs={{0,16},{8,24},{16,32},{24,40},{32,48},{40,56},{48,64},{56,72},{64,... | collective-permute-start | bytes 786440 | tf_op jit(solution)/shard_map/ppermute | solution.py:13
  116.3 18.6 %collective-permute-start.3 = (bf16[64,4,64,8]{0,1,3,2:T(4,128)(2,1)S(1)}, bf16[64,4,64,8]{0,1,3,2:T(4,128)(2,1)S(1)}, u32[]{:S(2)}, u32[]{:S(2)}) collective-permute-start(bf16[64,4,64,8]{0,1,3,2:T(4,128)(2,1)S(1)} %fusion.7), channel_id=1, source_target_pairs={{16,0},{24,8},{32,16},{40,24},{48,32},{56,40},{64,48},{72,56},{80,... | collective-permute-start | bytes 786440 | tf_op jit(solution)/shard_map/ppermute | solution.py:13
